TPU v7x, 256 devices: a whole 4x4x8 slice. The times are simulated.
256 devices in a mesh: ctx: 32 (over y, x, core), head: 8 (over z).
Axes of the slice: x: 4, y: 4, z: 8, core: 2. Of those that a mesh axis runs over, the one named last changes fastest.
Arguments:
- queries: bfloat16 [8192, 4096], P('ctx', 'head'), may hold values from -6 to 6
- key_rows: bfloat16 [8192, 4096], P('ctx', 'head'), may hold values from -6 to 6
- values: bfloat16 [8192, 4096], P('ctx', 'head'), may hold values from -6 to 6
- log_decay: float32 [8192, 32], P('ctx', 'head'), may hold values from 0 to 1, as said below
- head_gain: bfloat16 [4096], P('head'), may hold values from 0.099609375 to 1.8984375
- out_weight: bfloat16 [3072, 4096], P('ctx', 'head'), may hold values from -0.09375 to 0.09375
- residual: bfloat16 [8192, 3072], P('ctx', 'head'), may hold values from -6 to 6
- norm_gain: bfloat16 [3072], P('head'), may hold values from 0.099609375 to 1.8984375
- router: bfloat16 [3072, 32], replicated, may hold values from -0.21875 to 0.21875
- expert_ids: int32 [8192, 2], P('ctx'), may hold values from 0 to 31, all different within a row; in each aligned block of 256 rows (0 to 255, 256 to 511, ...) at most 24 rows name the same one
- gate_weight: bfloat16 [32, 3072, 5120], P('ctx', None, 'head'), may hold values from -0.109375 to 0.109375
- up_weight: bfloat16 [32, 3072, 5120], P('ctx', None, 'head'), may hold values from -0.109375 to 0.109375
- down_weight: bfloat16 [32, 5120, 3072], P('ctx', 'head'), may hold values from -0.125 to 0.125
Outputs:
- layer_out: float32 [8192, 3072], P('ctx', 'head')
Inputs may be any that keep to these rules, and one draw needn't show every extreme that they name: `log_decay`: amounts by which a head's state decays at a position: the state is multiplied by exp(-value). `expert_ids`: each row names 2 different experts; among the rows of one block of 256 positions no expert is named more than 24 times, a bound that some block reaches.
All inputs are finite; a program needn't handle non-finite values.
Results may differ from a plain program's by a relative error of at most 0.007.
Values may be sent and summed in bfloat16 or wider, within the bound.
No kernel may reach another device: no remote copies, remote signals or barrier semaphores. Data moves between devices by JAX's collectives and lax.ppermute only.
A program may use at most 128 MiB of HBM per device.

v0:
```python
import jax
import jax.numpy as jnp
from jax import lax
from jax.sharding import PartitionSpec as P

HEAD_DIM = 128
TOP = 2


HIGH = lax.Precision.HIGHEST
EPSILON = 1e-05


def combine(earlier, later):
    rows = HEAD_DIM
    decay_late = later[:, rows:rows + 1, 0:1]
    state = decay_late * earlier[:, :rows] + later[:, :rows]
    decay = earlier[:, rows:rows + 1] * later[:, rows:rows + 1]
    pad = jnp.zeros((later.shape[0], later.shape[1] - rows - 1, later.shape[2]), later.dtype)
    return jnp.concatenate([state, decay, pad], axis=1)


def exclusive_scan(packed, axis):
    count, mine = lax.axis_size(axis), lax.axis_index(axis)
    rows = HEAD_DIM
    identity = jnp.zeros_like(packed).at[:, rows].set(1.0)
    window = packed
    before = identity
    shift = 1
    while shift < count:
        pairs = [(j, j + shift) for j in range(count - shift)]
        got = lax.ppermute(window, axis, pairs)
        got = jnp.where(mine >= shift, got, identity)
        before = combine(got, before)
        if 2 * shift < count:
            window = combine(got, window)
        shift *= 2
    return before[:, :rows]


def on_device(
    queries,
    key_rows,
    values,
    log_decay,
    head_gain,
    out_weight,
    residual,
    norm_gain,
    router,
    expert_ids,
    gate_weight,
    up_weight,
    down_weight,
):
    rows = queries.shape[0]
    heads_here = log_decay.shape[1]
    groups = lax.axis_size("head")
    query_heads = queries.reshape(rows, heads_here, HEAD_DIM)
    key_heads = key_rows.reshape(rows, heads_here, HEAD_DIM)
    value_heads = values.reshape(rows, heads_here, HEAD_DIM)
    cumulative = jnp.cumsum(log_decay, axis=0)
    scores = jnp.einsum("thd,jhd->htj", query_heads, key_heads, preferred_element_type=jnp.float32)
    causal = jnp.arange(rows)[:, None] >= jnp.arange(rows)[None, :]
    gap = cumulative.T[:, :, None] - cumulative.T[:, None, :]
    weight = jnp.where(causal[None], jnp.exp(-jnp.where(causal[None], gap, 0.0)), 0.0)
    weighted = (scores * weight).astype(jnp.bfloat16)
    inner = jnp.einsum("htj,jhd->thd", weighted, value_heads, preferred_element_type=jnp.float32)
    value_wide = value_heads.astype(jnp.float32)
    tail = jnp.exp(cumulative - cumulative[-1:])
    keys_tail = key_heads.astype(jnp.float32) * tail[:, :, None]
    local_state = jnp.einsum("jhd,jhe->hde", keys_tail, value_wide, precision=HIGH)
    shard_decay = jnp.exp(-cumulative[-1])
    decay_rows = jnp.broadcast_to(shard_decay[:, None, None], (heads_here, 1, HEAD_DIM))
    pad = jnp.zeros((heads_here, 7, HEAD_DIM), jnp.float32)
    packed = jnp.concatenate([local_state, decay_rows, pad], axis=1)
    incoming = exclusive_scan(packed, "ctx")
    query_decayed = query_heads.astype(jnp.float32) * jnp.exp(-cumulative)[:, :, None]
    outer = jnp.einsum("thd,hde->the", query_decayed, incoming, precision=HIGH)
    mixed = inner + outer
    mean_sq = jnp.mean(mixed * mixed, axis=-1, keepdims=True)
    gain_heads = head_gain.astype(jnp.float32).reshape(heads_here, HEAD_DIM)
    normed = (
        (mixed * lax.rsqrt(mean_sq + EPSILON) * gain_heads)
        .astype(jnp.bfloat16)
        .reshape(rows, heads_here * HEAD_DIM)
    )
    width = residual.shape[1]
    full = width * groups
    weight_all = lax.all_gather(out_weight, "ctx", axis=0, tiled=True).reshape(
        groups, width, heads_here * HEAD_DIM
    )
    partial_proj = jnp.einsum(
        "tk,gck->gtc", normed, weight_all, preferred_element_type=jnp.float32
    ).astype(jnp.bfloat16)
    total = lax.psum_scatter(partial_proj, "head", scatter_dimension=0, tiled=True)
    stream_mine = residual.astype(jnp.float32) + total[0].astype(jnp.float32)
    sq_part = jnp.sum(stream_mine * stream_mine, axis=1)
    sq_hi = sq_part.astype(jnp.bfloat16)
    sq_lo = (sq_part - sq_hi.astype(jnp.float32)).astype(jnp.bfloat16)
    experts = router.shape[1]
    capacity = 3 * rows * TOP // (2 * experts)
    lane = 128
    wide = width + lane
    other_id = expert_ids[:, ::-1].astype(jnp.bfloat16)
    token_rows = jnp.concatenate(
        [
            stream_mine.astype(jnp.bfloat16),
            sq_hi[:, None],
            sq_lo[:, None],
            jnp.zeros((rows, lane - 2), jnp.bfloat16),
        ],
        axis=1,
    )
    token_rows = jnp.concatenate([token_rows, jnp.zeros((8, wide), jnp.bfloat16)], axis=0)
    flat_ids = expert_ids.reshape(-1)
    onehot = (flat_ids[:, None] == jnp.arange(experts, dtype=jnp.int32)[None, :]).astype(jnp.int32)
    before = jnp.cumsum(onehot, axis=0) - onehot
    position = jnp.sum(before * onehot, axis=1)
    slot = flat_ids * capacity + position
    owner = jnp.arange(rows * TOP, dtype=jnp.int32) // TOP
    slot_token = jnp.full((experts * capacity,), rows, jnp.int32).at[slot].set(owner)
    slot_other = jnp.zeros((experts * capacity,), jnp.bfloat16).at[slot].set(other_id.reshape(-1))
    outgoing = token_rows[slot_token]
    outgoing = outgoing.at[:, width + 2].set(slot_other).reshape(experts, capacity, wide)
    arriving = lax.all_to_all(outgoing, "ctx", split_axis=0, concat_axis=0, tiled=True)
    flat = arriving.reshape(-1, wide)
    gain_row = jnp.concatenate([norm_gain, jnp.zeros((lane,), jnp.bfloat16)])
    gain_rows = jnp.zeros((8, wide), jnp.bfloat16).at[0].set(gain_row)
    gathered = lax.all_gather(jnp.concatenate([flat, gain_rows], axis=0), "head", axis=0)
    slots_here = flat.shape[0]
    stream_blocks = gathered[:, :slots_here, :width].astype(jnp.float32)
    gain_blocks = gathered[:, slots_here, :width].astype(jnp.float32)
    sq_parts = gathered[:, :slots_here, width:width + 2].astype(jnp.float32)
    stream_sq = jnp.sum(sq_parts, axis=(0, 2))[None, :, None] / full
    other_here = flat[:, width + 2].astype(jnp.int32)
    moe_in = (stream_blocks * lax.rsqrt(stream_sq + EPSILON) * gain_blocks[:, None, :]).astype(
        jnp.bfloat16
    )
    router_blocks = router.reshape(groups, width, router.shape[1])
    logits = jnp.einsum("grc,gce->re", moe_in, router_blocks, preferred_element_type=jnp.float32)
    expert_here = lax.axis_index("ctx")
    names = jnp.arange(experts, dtype=jnp.int32)[None, :]
    own_logit = jnp.sum(jnp.where(names == expert_here, logits, 0.0), axis=1)
    other_logit = jnp.sum(jnp.where(names == other_here[:, None], logits, 0.0), axis=1)
    mix_here = jax.nn.sigmoid(own_logit - other_logit)
    mix_hi = mix_here.astype(jnp.bfloat16)
    mix_lo = (mix_here - mix_hi.astype(jnp.float32)).astype(jnp.bfloat16)
    hidden = gate_weight.shape[2]
    gate = jnp.einsum(
        "grc,gcf->rf", moe_in, gate_weight[0].reshape(groups, width, hidden),
        preferred_element_type=jnp.float32,
    )
    up = jnp.einsum(
        "grc,gcf->rf", moe_in, up_weight[0].reshape(groups, width, hidden),
        preferred_element_type=jnp.float32,
    )
    activated = (jax.nn.silu(gate) * up).astype(jnp.bfloat16)
    down = down_weight[0].reshape(down_weight.shape[1], groups, width)
    partial_value = jnp.einsum(
        "rf,fgc->grc", activated, down, preferred_element_type=jnp.float32
    ).astype(jnp.bfloat16)
    summed = lax.psum_scatter(partial_value, "head", scatter_dimension=0, tiled=True)[0]
    back = jnp.concatenate(
        [
            summed,
            mix_hi[:, None],
            mix_lo[:, None],
            jnp.zeros((slots_here, lane - 2), jnp.bfloat16),
        ],
        axis=1,
    ).reshape(arriving.shape[0], arriving.shape[1], wide)
    returned = lax.all_to_all(back, "ctx", split_axis=0, concat_axis=0, tiled=True)
    picked_rows = returned.reshape(experts * capacity, wide)[slot].astype(jnp.float32)
    picked_rows = picked_rows.reshape(rows, TOP, wide)
    mix_weights = picked_rows[:, :, width] + picked_rows[:, :, width + 1]
    moe_out = jnp.sum(picked_rows[:, :, :width] * mix_weights[:, :, None], axis=1)
    return stream_mine + moe_out


def solution(mesh):
    placed = (
        P("ctx", "head"),
        P("ctx", "head"),
        P("ctx", "head"),
        P("ctx", "head"),
        P("head"),
        P("ctx", "head"),
        P("ctx", "head"),
        P("head"),
        P(),
        P("ctx", None),
        P("ctx", None, "head"),
        P("ctx", None, "head"),
        P("ctx", "head", None),
    )
    return jax.shard_map(
        on_device, mesh=mesh, in_specs=placed, out_specs=P("ctx", "head"), check_vma=False
    )
```

profile of v0, /device:TPU:1, one launch (start us, length us, event | category | flops | bytes accessed | tf_op | source)
XLA Modules:
  0.0 334.5 jit_solution(13303171259257911316)
XLA Ops:
  11.9 4.5 %collective-permute-start = (f32[4,136,128]{2,1,0:T(8,128)S(1)}, f32[4,136,128]{2,1,0:T(8,128)S(1)}, u32[]{:S(2)}, u32[]{:S(2)}) collective-permute-start(f32[4,136,128]{2,1,0:T(8,128)S(1)} %maximum_maximum_fusion.1), channel_id=1, source_target_pairs={{0,8},{8,16},{16,24},{24,32},{32,40},{40,48},{48,56},{56,64},{64,7... | collective-permute-start | bytes 835592 | tf_op jit(solution)/shard_map/ppermute | solution.py:32
  16.5 3.4 %collective-permute-done = f32[4,136,128]{2,1,0:T(8,128)S(1)} collective-permute-done((f32[4,136,128]{2,1,0:T(8,128)S(1)}, f32[4,136,128]{2,1,0:T(8,128)S(1)}, u32[]{:S(2)}, u32[]{:S(2)}) %collective-permute-start) | collective-permute-done | bytes 278560 | tf_op jit(solution)/shard_map/ppermute | solution.py:32
  23.5 4.4 %collective-permute-done.1 = f32[4,136,128]{2,1,0:T(8,128)S(1)} collective-permute-done((f32[4,136,128]{2,1,0:T(8,128)S(1)}, f32[4,136,128]{2,1,0:T(8,128)S(1)}, u32[]{:S(2)}, u32[]{:S(2)}) %collective-permute-start.1) | collective-permute-done | bytes 278560 | tf_op jit(solution)/shard_map/ppermute | solution.py:32
  28.2 5.1 %collective-permute-start.2 = (f32[4,136,128]{2,1,0:T(8,128)S(1)}, f32[4,136,128]{2,1,0:T(8,128)S(1)}, u32[]{:S(2)}, u32[]{:S(2)}) collective-permute-start(f32[4,136,128]{2,1,0:T(8,128)S(1)} %maximum_maximum_fusion.3), channel_id=1, source_target_pairs={{0,32},{8,40},{16,48},{24,56},{32,64},{40,72},{48,80},{56,88},{64,... | collective-permute-start | bytes 835592 | tf_op jit(solution)/shard_map/ppermute | solution.py:32
  34.0 3.2 collective-permute-done.2
  37.5 5.9 %collective-permute-start.3 = (f32[4,136,128]{2,1,0:T(8,128)S(1)}, f32[4,136,128]{2,1,0:T(8,128)S(1)}, u32[]{:S(2)}, u32[]{:S(2)}) collective-permute-start(f32[4,136,128]{2,1,0:T(8,128)S(1)} %maximum_maximum_fusion.4), channel_id=1, source_target_pairs={{0,64},{8,72},{16,80},{24,88},{32,96},{40,104},{48,112},{56,120},{... | collective-permute-start | bytes 835592 | tf_op jit(solution)/shard_map/ppermute | solution.py:32
  43.6 3.9 %collective-permute-done.3 = f32[4,136,128]{2,1,0:T(8,128)S(1)} collective-permute-done((f32[4,136,128]{2,1,0:T(8,128)S(1)}, f32[4,136,128]{2,1,0:T(8,128)S(1)}, u32[]{:S(2)}, u32[]{:S(2)}) %collective-permute-start.3) | collective-permute-done | bytes 278560 | tf_op jit(solution)/shard_map/ppermute | solution.py:32
  47.7 5.4 %collective-permute-start.4 = (f32[4,136,128]{2,1,0:T(8,128)S(1)}, f32[4,136,128]{2,1,0:T(8,128)S(1)}, u32[]{:S(2)}, u32[]{:S(2)}) collective-permute-start(f32[4,136,128]{2,1,0:T(8,128)S(1)} %maximum_maximum_fusion.5), channel_id=1, source_target_pairs={{0,128},{8,136},{16,144},{24,152},{32,160},{40,168},{48,176},{56,1... | collective-permute-start | bytes 835592 | tf_op jit(solution)/shard_map/ppermute | solution.py:32
  57.6 15.2 %all-gather.4.cloned.1.call-done = bf16[3072,512]{1,0:T(8,128)(2,1)} async-done(((bf16[96,512]{1,0:T(8,128)(2,1)}), bf16[3072,512]{1,0:T(8,128)(2,1)}) %all-gather.4.cloned.1.call-update) | async-done | bytes 3145744 | tf_op jit(solution)/shard_map/all_gather | solution.py:90
  72.8 4.1 %fusion.9 = bf16[8,256,384]{2,1,0:T(8,128)(2,1)} fusion(bf16[256,512,1]{0,1,2:T(8,128)(2,1)S(1)} %bitcast.151, bf16[8,384,512]{2,1,0:T(8,128)(2,1)} %bitcast.150), kind=kOutput, calls=%fused_computation.19 | convolution fusion | flops 806092800 | bytes 4980736 | tf_op jit(solution)/shard_map/tk,gck->gtc/dot_general | solution.py:93
  79.7 3.8 %scatter_custom_fusion.1 = bf16[768]{0:T(1024)(128)(2,1)S(1)} fusion(s32[512]{0:T(512)S(1)} %bitcast.169, bf16[512]{0:T(512)(128)(2,1)S(1)} %reshape.370, bf16[]{:T(256)} %constant.152.clone.1), kind=kCustom, calls=%fused_computation.151 | custom fusion | bytes 1538 | tf_op jit(solution)/shard_map/scatter | solution.py:123
  86.5 27.3 %reduce-scatter.3.cloned.1.call-done = bf16[1,256,384]{2,1,0:T(8,128)(2,1)} async-done(((bf16[8,256,384]{2,1,0:T(8,128)(2,1)}), bf16[1,256,384]{2,1,0:T(8,128)(2,1)}) %reduce-scatter.3.cloned.1.call-update) | async-done | bytes 196624 | tf_op jit(solution)/shard_map/reduce_scatter | solution.py:96
  115.4 3.3 gather_fusion
  122.8 11.6 %all-to-all-start = ((bf16[32,24,512]{2,1,0:T(8,128)(2,1)}), bf16[32,24,512]{2,1,0:T(8,128)(2,1)S(1)}, u32[]{:S(2)}, u32[]{:S(2)}) async-start(bf16[32,24,512]{2,1,0:T(8,128)(2,1)} %bitcast.15), calls=%async_computation.1 | async-start | bytes 1572864 | tf_op jit(solution)/shard_map/all_to_all | solution.py:126
  134.5 14.2 %all-to-all-done = bf16[32,24,512]{2,1,0:T(8,128)(2,1)S(1)} async-done(((bf16[32,24,512]{2,1,0:T(8,128)(2,1)}), bf16[32,24,512]{2,1,0:T(8,128)(2,1)S(1)}, u32[]{:S(2)}, u32[]{:S(2)}) %all-to-all-start) | async-done | bytes 786464 | tf_op jit(solution)/shard_map/all_to_all | solution.py:126
  149.7 5.0 %copy.150 = bf16[80,8,8,384]{3,2,1,0:T(8,128)(2,1)} copy(bf16[80,8,8,384]{3,1,2,0:T(8,128)(2,1)} %bitcast.148) | data formatting | bytes 7864320
  154.7 65.0 %all-gather.6.cloned.1.call-done = bf16[6208,512]{1,0:T(8,128)(2,1)} async-done(((bf16[776,512]{1,0:T(8,128)(2,1)}), bf16[6208,512]{1,0:T(8,128)(2,1)}) %all-gather.6.cloned.1.call-update) | async-done | bytes 6357008 | tf_op jit(solution)/shard_map/all_gather | solution.py:130
  222.5 7.3 %fusion.78 = f32[768,640,1]{1,0,2:T(8,128)S(1)} fusion(bf16[8,384,640]{2,1,0:T(8,128)(2,1)} %bitcast.175, bf16[8,776,512]{2,1,0:T(8,128)(2,1)} %bitcast.157, f32[8,384]{1,0:T(8,128)S(1)} %bitcast.162, f32[768]{0:T(1024)S(1)} %add_rsqrt_fusion), kind=kOutput, calls=%fused_computation.160 | convolution fusion | flops 3029336064 | bytes 10632192 | tf_op jit(solution)/shard_map/grc,gcf->rf/dot_general | solution.py:150
  229.8 4.0 %fusion.10 = bf16[768,640,1]{1,0,2:T(8,128)(2,1)S(1)} fusion(bf16[8,384,640]{2,1,0:T(8,128)(2,1)S(1)} %bitcast.176, f32[768,640,1]{1,0,2:T(8,128)S(1)} %fusion.78, bf16[8,776,512]{2,1,0:T(8,128)(2,1)S(1)} %bitcast.161, f32[8,384]{1,0:T(8,128)S(1)} %bitcast.163, f32[768]{0:T(1024)S(1)} %add_rsqrt_fusion), kind=kOutput, calls=%fused_computation.21 | convolution fusion | flops 3032285184 | bytes 11616256 | tf_op jit(solution)/shard_map/grc,gcf->rf/dot_general | solution.py:154
  233.9 5.6 %convert_bitcast_fusion = bf16[8,768,384]{2,1,0:T(8,128)(2,1)} fusion(bf16[768,640,1]{1,0,2:T(8,128)(2,1)S(1)} %fusion.10, bf16[640,8,384]{2,1,0:T(8,128)(2,1)S(1)} %bitcast.149), kind=kOutput, calls=%fused_computation.5 | convolution fusion | flops 3022258176 | bytes 9633792 | tf_op jit(solution)/shard_map/rf,fgc->grc/dot_general | solution.py:160
  240.4 4.0 %select_reduce_fusion = (f32[768]{0:T(1024)S(1)}, f32[768]{0:T(1024)S(1)}) fusion(s32[768]{0:T(1024)S(1)} %convert_reduce_fusion.1, pred[32]{0:T(512)(128)(4,1)S(1)} %iota_compare_fusion.5, bf16[4,8,8,384]{3,2,1,0:T(8,128)(2,1)S(1)} %bitcast.177, bf16[8,776,512]{2,1,0:T(8,128)(2,1)} %bitcast.158, f32[8,384]{1,0:T(8,128)S(1)} %bitcast.164, ...), kind=kOutput, calls=%fused_computation.99 | convolution fusion | flops 160553472 | bytes 4939808 | tf_op jit(solution)/shard_map/grc,gce->re/dot_general | solution.py:141
  245.2 53.5 %reduce-scatter.5.cloned.1.call-done = bf16[1,768,384]{2,1,0:T(8,128)(2,1)} async-done(((bf16[8,768,384]{2,1,0:T(8,128)(2,1)}), bf16[1,768,384]{2,1,0:T(8,128)(2,1)}) %reduce-scatter.5.cloned.1.call-update) | async-done | bytes 589840 | tf_op jit(solution)/shard_map/reduce_scatter | solution.py:163
  300.9 7.6 %all-to-all-start.1 = ((bf16[32,24,512]{2,1,0:T(8,128)(2,1)}), bf16[32,24,512]{2,1,0:T(8,128)(2,1)S(1)}, u32[]{:S(2)}, u32[]{:S(2)}) async-start(bf16[32,24,512]{2,1,0:T(8,128)(2,1)} %maximum_maximum_fusion), calls=%async_computation.3 | async-start | bytes 1572864 | tf_op jit(solution)/shard_map/all_to_all | solution.py:173
  308.5 14.2 %all-to-all-done.1 = bf16[32,24,512]{2,1,0:T(8,128)(2,1)S(1)} async-done(((bf16[32,24,512]{2,1,0:T(8,128)(2,1)}), bf16[32,24,512]{2,1,0:T(8,128)(2,1)S(1)}, u32[]{:S(2)}, u32[]{:S(2)}) %all-to-all-start.1) | async-done | bytes 786464 | tf_op jit(solution)/shard_map/all_to_all | solution.py:173
  (142 shorter events, 39.1 us)
Async XLA Ops:
  6.5 26.8 %copy-start = (bf16[256,512]{1,0:T(8,128)(2,1)S(1)}, bf16[256,512]{1,0:T(8,128)(2,1)}, u32[]{:S(2)}) copy-start(bf16[256,512]{1,0:T(8,128)(2,1)} %param.19) | copy-start | bytes 786436
  6.5 21.4 %copy-start.1 = (f32[4,136,128]{2,1,0:T(8,128)S(1)}, f32[4,136,128]{2,1,0:T(8,128)}, u32[]{:S(2)}) copy-start(f32[4,136,128]{2,1,0:T(8,128)} %constant.147.clone.1) | copy-start | bytes 835588
  6.5 26.8 %copy-start.5 = (bf16[256,512]{1,0:T(8,128)(2,1)S(1)}, bf16[256,512]{1,0:T(8,128)(2,1)}, u32[]{:S(2)}) copy-start(bf16[256,512]{1,0:T(8,128)(2,1)} %param.21) | copy-start | bytes 786436
  6.5 66.2 %all-gather.4.cloned.1.call-start = ((), (), s32[]{:S(2)}) async-start(), calls=%async_computation.4 | async-start | bytes 3244032 | tf_op jit(solution)/shard_map/all_gather | solution.py:90
  11.9 8.0 %collective-permute-start = (f32[4,136,128]{2,1,0:T(8,128)S(1)}, f32[4,136,128]{2,1,0:T(8,128)S(1)}, u32[]{:S(2)}, u32[]{:S(2)}) collective-permute-start(f32[4,136,128]{2,1,0:T(8,128)S(1)} %maximum_maximum_fusion.1), channel_id=1, source_target_pairs={{0,8},{8,16},{16,24},{24,32},{32,40},{40,48},{48,56},{56,64},{64,7... | collective-permute-start | bytes 835592 | tf_op jit(solution)/shard_map/ppermute | solution.py:32
  16.4 97.5 %reduce-scatter.3.cloned.1.call-start = ((), (), s32[]{:S(2)}) async-start(), calls=%async_computation.5 | async-start | bytes 1769472 | tf_op jit(solution)/shard_map/reduce_scatter | solution.py:96
  20.2 23.3 %copy-start.7 = (bf16[512]{0:T(512)(128)(2,1)S(1)}, bf16[512]{0:T(512)(128)(2,1)}, u32[]{:S(2)}) copy-start(bf16[512]{0:T(512)(128)(2,1)} %param.23) | copy-start | bytes 3076
  20.2 7.7 %collective-permute-start.1 = (f32[4,136,128]{2,1,0:T(8,128)S(1)}, f32[4,136,128]{2,1,0:T(8,128)S(1)}, u32[]{:S(2)}, u32[]{:S(2)}) collective-permute-start(f32[4,136,128]{2,1,0:T(8,128)S(1)} %maximum_maximum_fusion.2), channel_id=1, source_target_pairs={{0,16},{8,24},{16,32},{24,40},{32,48},{40,56},{48,64},{56,72},{64,... | collective-permute-start | bytes 835592 | tf_op jit(solution)/shard_map/ppermute | solution.py:32
  28.2 9.1 %collective-permute-start.2 = (f32[4,136,128]{2,1,0:T(8,128)S(1)}, f32[4,136,128]{2,1,0:T(8,128)S(1)}, u32[]{:S(2)}, u32[]{:S(2)}) collective-permute-start(f32[4,136,128]{2,1,0:T(8,128)S(1)} %maximum_maximum_fusion.3), channel_id=1, source_target_pairs={{0,32},{8,40},{16,48},{24,56},{32,64},{40,72},{48,80},{56,88},{64,... | collective-permute-start | bytes 835592 | tf_op jit(solution)/shard_map/ppermute | solution.py:32
  37.5 9.9 %collective-permute-start.3 = (f32[4,136,128]{2,1,0:T(8,128)S(1)}, f32[4,136,128]{2,1,0:T(8,128)S(1)}, u32[]{:S(2)}, u32[]{:S(2)}) collective-permute-start(f32[4,136,128]{2,1,0:T(8,128)S(1)} %maximum_maximum_fusion.4), channel_id=1, source_target_pairs={{0,64},{8,72},{16,80},{24,88},{32,96},{40,104},{48,112},{56,120},{... | collective-permute-start | bytes 835592 | tf_op jit(solution)/shard_map/ppermute | solution.py:32
  47.7 8.9 %collective-permute-start.4 = (f32[4,136,128]{2,1,0:T(8,128)S(1)}, f32[4,136,128]{2,1,0:T(8,128)S(1)}, u32[]{:S(2)}, u32[]{:S(2)}) collective-permute-start(f32[4,136,128]{2,1,0:T(8,128)S(1)} %maximum_maximum_fusion.5), channel_id=1, source_target_pairs={{0,128},{8,136},{16,144},{24,152},{32,160},{40,168},{48,176},{56,1... | collective-permute-start | bytes 835592 | tf_op jit(solution)/shard_map/ppermute | solution.py:32
  57.4 19.4 %copy-start.6 = (s32[256,2]{0,1:T(2,128)S(1)}, s32[256,2]{0,1:T(2,128)}, u32[]{:S(2)}) copy-start(s32[256,2]{0,1:T(2,128)} %param.28) | copy-start | bytes 6148
  57.6 56.3 %copy-start.3 = (bf16[256,384]{1,0:T(8,128)(2,1)S(1)}, bf16[256,384]{1,0:T(8,128)(2,1)}, u32[]{:S(2)}) copy-start(bf16[256,384]{1,0:T(8,128)(2,1)} %param.25) | copy-start | bytes 589828
  115.4 19.0 %copy-start.8 = (bf16[384]{0:T(512)(128)(2,1)S(1)}, bf16[384]{0:T(512)(128)(2,1)}, u32[]{:S(2)}) copy-start(bf16[384]{0:T(512)(128)(2,1)} %param.26) | copy-start | bytes 2308
  122.8 25.9 %all-to-all-start = ((bf16[32,24,512]{2,1,0:T(8,128)(2,1)}), bf16[32,24,512]{2,1,0:T(8,128)(2,1)S(1)}, u32[]{:S(2)}, u32[]{:S(2)}) async-start(bf16[32,24,512]{2,1,0:T(8,128)(2,1)} %bitcast.15), calls=%async_computation.1 | async-start | bytes 1572864 | tf_op jit(solution)/shard_map/all_to_all | solution.py:126
  134.4 85.3 %all-gather.6.cloned.1.call-start = ((), (), s32[]{:S(2)}) async-start(), calls=%async_computation.7 | async-start | bytes 7151616 | tf_op jit(solution)/shard_map/all_gather | solution.py:130
  149.6 149.1 %reduce-scatter.5.cloned.1.call-start = ((), (), s32[]{:S(2)}) async-start(), calls=%async_computation.6 | async-start | bytes 5308416 | tf_op jit(solution)/shard_map/reduce_scatter | solution.py:163
  220.5 9.3 %slice-start = ((s8[6356992]{0:T(1024)(128)(4,1)}), s8[4194304]{0:T(1024)(128)(4,1)S(1)}, s32[]{:S(2)}) async-start(s8[6356992]{0:T(1024)(128)(4,1)} %bitcast.159), calls=%async_computation.8 | async-start | bytes 8388608
  222.5 7.3 %slice-start.1 = ((s8[6356992]{0:T(1024)(128)(4,1)}), s8[2162688]{0:T(1024)(128)(4,1)S(1)}, s32[]{:S(2)}) async-start(s8[6356992]{0:T(1024)(128)(4,1)} %bitcast.159), calls=%async_computation.9 | async-start | bytes 4325376
  222.5 7.3 %copy-start.9 = (bf16[1,3072,640]{2,1,0:T(8,128)(2,1)S(1)}, bf16[1,3072,640]{2,1,0:T(8,128)(2,1)}, u32[]{:S(2)}) copy-start(bf16[1,3072,640]{2,1,0:T(8,128)(2,1)} %param.30) | copy-start | bytes 11796484
  229.8 4.1 %copy-start.2 = (bf16[80,8,8,384]{3,2,1,0:T(8,128)(2,1)S(1)}, bf16[80,8,8,384]{3,2,1,0:T(8,128)(2,1)}, u32[]{:S(2)}) copy-start(bf16[80,8,8,384]{3,2,1,0:T(8,128)(2,1)} %copy.150) | copy-start | bytes 11796484
  239.5 0.9 copy-start.10
  300.9 21.9 %all-to-all-start.1 = ((bf16[32,24,512]{2,1,0:T(8,128)(2,1)}), bf16[32,24,512]{2,1,0:T(8,128)(2,1)S(1)}, u32[]{:S(2)}, u32[]{:S(2)}) async-start(bf16[32,24,512]{2,1,0:T(8,128)(2,1)} %maximum_maximum_fusion), calls=%async_computation.3 | async-start | bytes 1572864 | tf_op jit(solution)/shard_map/all_to_all | solution.py:173
  322.7 4.4 %copy-start.4 = (bf16[1,256,384]{2,1,0:T(8,128)(2,1)S(1)}, bf16[1,256,384]{2,1,0:T(8,128)(2,1)}, u32[]{:S(2)}) copy-start(bf16[1,256,384]{2,1,0:T(8,128)(2,1)} %reduce-scatter.3.cloned.1.call-done) | copy-start | bytes 589828
Sparse Core Ops, SparseCore 0:
  16.5 56.1 all-gather.3
  77.0 36.8 reduce-scatter.2
  149.7 69.9 all-gather.5
  239.7 58.9 reduce-scatter.4
where the time goes:
time: 335 us; the launch traced here: 334 us
  waiting for transfers between devices  207 us (62%)
  starting transfers between devices  43.4 us (13%)
  matrix products  27.7 us (8%)
  local copies, waits for them, and re-layouts  26.3 us (8%)
  other arithmetic  15.7 us (5%)
  between operations  13.8 us (4%)
    all_gather x1, waiting for transfers between devices, on_device(): lax.all_gather(jnp.concatenate([flat, gain_rows], axis=0), 'head', axis=0)  65 us
    reduce_scatter x1, waiting for transfers between devices, on_device(): lax.psum_scatter(partial_value, 'head', scatter_dimension=0, tiled=True)[0]  53.5 us
    reduce_scatter x1, waiting for transfers between devices, on_device(): lax.psum_scatter(partial_proj, 'head', scatter_dimension=0, tiled=True)  27.3 us
    ppermute x5, starting transfers between devices, exclusive_scan(): got = lax.ppermute(window, axis, pairs)  24.1 us
    ppermute x5, waiting for transfers between devices, exclusive_scan(): got = lax.ppermute(window, axis, pairs)  18 us
    all_gather x1, waiting for transfers between devices, on_device(): lax.all_gather(out_weight, 'ctx', axis=0, tiled=True)  15.2 us
    all_to_all x1, waiting for transfers between devices, on_device(): lax.all_to_all(back, 'ctx', split_axis=0, concat_axis=0, tiled=True)  14.2 us
    all_to_all x1, waiting for transfers between devices, on_device(): lax.all_to_all(outgoing, 'ctx', split_axis=0, concat_axis=0, tiled=True)  14.2 us
  transfers between devices with their start and end apart: 11, of which 11 were waited for; matrix products, arithmetic and copies ran while one was open for 7% of the time, Pallas kernels for 0%

commit v1 on v0

--- a/solution.py
+++ b/solution.py
@@ -125,14 +125,18 @@
     outgoing = outgoing.at[:, width + 2].set(slot_other).reshape(experts, capacity, wide)
     arriving = lax.all_to_all(outgoing, "ctx", split_axis=0, concat_axis=0, tiled=True)
     flat = arriving.reshape(-1, wide)
-    gain_row = jnp.concatenate([norm_gain, jnp.zeros((lane,), jnp.bfloat16)])
-    gain_rows = jnp.zeros((8, wide), jnp.bfloat16).at[0].set(gain_row)
-    gathered = lax.all_gather(jnp.concatenate([flat, gain_rows], axis=0), "head", axis=0)
     slots_here = flat.shape[0]
-    stream_blocks = gathered[:, :slots_here, :width].astype(jnp.float32)
-    gain_blocks = gathered[:, slots_here, :width].astype(jnp.float32)
-    sq_parts = gathered[:, :slots_here, width:width + 2].astype(jnp.float32)
-    stream_sq = jnp.sum(sq_parts, axis=(0, 2))[None, :, None] / full
+    sq_rows = jnp.transpose(flat[:, width:width + 2]).reshape(2 * slots_here // width, width)
+    spare = 7 - sq_rows.shape[0]
+    extra = jnp.concatenate(
+        [norm_gain[None, :], sq_rows, jnp.zeros((spare, width), jnp.bfloat16)], axis=0
+    )
+    gathered = lax.all_gather(jnp.concatenate([flat[:, :width], extra], axis=0), "head", axis=0)
+    stream_blocks = gathered[:, :slots_here].astype(jnp.float32)
+    gain_blocks = gathered[:, slots_here].astype(jnp.float32)
+    sq_parts = gathered[:, slots_here + 1 : slots_here + 1 + sq_rows.shape[0]].astype(jnp.float32)
+    sq_parts = sq_parts.reshape(groups, 2, slots_here)
+    stream_sq = jnp.sum(sq_parts, axis=(0, 1))[None, :, None] / full
     other_here = flat[:, width + 2].astype(jnp.int32)
     moe_in = (stream_blocks * lax.rsqrt(stream_sq + EPSILON) * gain_blocks[:, None, :]).astype(
         jnp.bfloat16

time: 335 us -> 320 us (0.955)
  waiting for transfers between devices: 207 us -> 193 us
    all_gather x1, waiting for transfers between devices: 65 us -> 50.2 us  [on_device(): lax.all_gather(jnp.concatenate([flat[:, :width], extra], axis=0), 'head',...]
where the time goes in v1:
time: 320 us; the launch traced here: 319 us
  waiting for transfers between devices  193 us (60%)
  starting transfers between devices  43.4 us (14%)
  matrix products  27.7 us (9%)
  local copies, waits for them, and re-layouts  26.6 us (8%)
  other arithmetic  14.7 us (5%)
  between operations  13.8 us (4%)
    reduce_scatter x1, waiting for transfers between devices, on_device(): lax.psum_scatter(partial_value, 'head', scatter_dimension=0, tiled=True)[0]  53.5 us
    all_gather x1, waiting for transfers between devices, on_device(): lax.all_gather(jnp.concatenate([flat[:, :width], extra], axis=0), 'head',...  50.2 us
    reduce_scatter x1, waiting for transfers between devices, on_device(): lax.psum_scatter(partial_proj, 'head', scatter_dimension=0, tiled=True)  27.3 us
    ppermute x5, starting transfers between devices, exclusive_scan(): got = lax.ppermute(window, axis, pairs)  24.1 us
    ppermute x5, waiting for transfers between devices, exclusive_scan(): got = lax.ppermute(window, axis, pairs)  18 us
    all_gather x1, waiting for transfers between devices, on_device(): lax.all_gather(out_weight, 'ctx', axis=0, tiled=True)  15.2 us
    all_to_all x1, waiting for transfers between devices, on_device(): lax.all_to_all(back, 'ctx', split_axis=0, concat_axis=0, tiled=True)  14.2 us
    all_to_all x1, waiting for transfers between devices, on_device(): lax.all_to_all(outgoing, 'ctx', split_axis=0, concat_axis=0, tiled=True)  14.1 us
  transfers between devices with their start and end apart: 11, of which 11 were waited for; matrix products, arithmetic and copies ran while one was open for 7% of the time, Pallas kernels for 0%

profile of v1, /device:TPU:1, one launch (start us, length us, event | category | flops | bytes accessed | tf_op | source)
XLA Modules:
  0.0 318.7 jit_solution(5503128526121776230)
XLA Ops:
  11.9 4.5 %collective-permute-start = (f32[4,136,128]{2,1,0:T(8,128)S(1)}, f32[4,136,128]{2,1,0:T(8,128)S(1)}, u32[]{:S(2)}, u32[]{:S(2)}) collective-permute-start(f32[4,136,128]{2,1,0:T(8,128)S(1)} %maximum_maximum_fusion.2), channel_id=1, source_target_pairs={{0,8},{8,16},{16,24},{24,32},{32,40},{40,48},{48,56},{56,64},{64,7... | collective-permute-start | bytes 835592 | tf_op jit(solution)/shard_map/ppermute | solution.py:32
  16.5 3.4 %collective-permute-done = f32[4,136,128]{2,1,0:T(8,128)S(1)} collective-permute-done((f32[4,136,128]{2,1,0:T(8,128)S(1)}, f32[4,136,128]{2,1,0:T(8,128)S(1)}, u32[]{:S(2)}, u32[]{:S(2)}) %collective-permute-start) | collective-permute-done | bytes 278560 | tf_op jit(solution)/shard_map/ppermute | solution.py:32
  23.5 4.4 %collective-permute-done.1 = f32[4,136,128]{2,1,0:T(8,128)S(1)} collective-permute-done((f32[4,136,128]{2,1,0:T(8,128)S(1)}, f32[4,136,128]{2,1,0:T(8,128)S(1)}, u32[]{:S(2)}, u32[]{:S(2)}) %collective-permute-start.1) | collective-permute-done | bytes 278560 | tf_op jit(solution)/shard_map/ppermute | solution.py:32
  28.2 5.1 %collective-permute-start.2 = (f32[4,136,128]{2,1,0:T(8,128)S(1)}, f32[4,136,128]{2,1,0:T(8,128)S(1)}, u32[]{:S(2)}, u32[]{:S(2)}) collective-permute-start(f32[4,136,128]{2,1,0:T(8,128)S(1)} %maximum_maximum_fusion.4), channel_id=1, source_target_pairs={{0,32},{8,40},{16,48},{24,56},{32,64},{40,72},{48,80},{56,88},{64,... | collective-permute-start | bytes 835592 | tf_op jit(solution)/shard_map/ppermute | solution.py:32
  34.0 3.2 %collective-permute-done.2 = f32[4,136,128]{2,1,0:T(8,128)S(1)} collective-permute-done((f32[4,136,128]{2,1,0:T(8,128)S(1)}, f32[4,136,128]{2,1,0:T(8,128)S(1)}, u32[]{:S(2)}, u32[]{:S(2)}) %collective-permute-start.2) | collective-permute-done | bytes 278560 | tf_op jit(solution)/shard_map/ppermute | solution.py:32
  37.5 5.9 %collective-permute-start.3 = (f32[4,136,128]{2,1,0:T(8,128)S(1)}, f32[4,136,128]{2,1,0:T(8,128)S(1)}, u32[]{:S(2)}, u32[]{:S(2)}) collective-permute-start(f32[4,136,128]{2,1,0:T(8,128)S(1)} %maximum_maximum_fusion.5), channel_id=1, source_target_pairs={{0,64},{8,72},{16,80},{24,88},{32,96},{40,104},{48,112},{56,120},{... | collective-permute-start | bytes 835592 | tf_op jit(solution)/shard_map/ppermute | solution.py:32
  43.6 3.9 %collective-permute-done.3 = f32[4,136,128]{2,1,0:T(8,128)S(1)} collective-permute-done((f32[4,136,128]{2,1,0:T(8,128)S(1)}, f32[4,136,128]{2,1,0:T(8,128)S(1)}, u32[]{:S(2)}, u32[]{:S(2)}) %collective-permute-start.3) | collective-permute-done | bytes 278560 | tf_op jit(solution)/shard_map/ppermute | solution.py:32
  47.7 5.4 %collective-permute-start.4 = (f32[4,136,128]{2,1,0:T(8,128)S(1)}, f32[4,136,128]{2,1,0:T(8,128)S(1)}, u32[]{:S(2)}, u32[]{:S(2)}) collective-permute-start(f32[4,136,128]{2,1,0:T(8,128)S(1)} %maximum_maximum_fusion.6), channel_id=1, source_target_pairs={{0,128},{8,136},{16,144},{24,152},{32,160},{40,168},{48,176},{56,1... | collective-permute-start | bytes 835592 | tf_op jit(solution)/shard_map/ppermute | solution.py:32
  57.6 15.2 %all-gather.4.cloned.1.call-done = bf16[3072,512]{1,0:T(8,128)(2,1)} async-done(((bf16[96,512]{1,0:T(8,128)(2,1)}), bf16[3072,512]{1,0:T(8,128)(2,1)}) %all-gather.4.cloned.1.call-update) | async-done | bytes 3145744 | tf_op jit(solution)/shard_map/all_gather | solution.py:90
  72.8 4.1 %fusion.8 = bf16[8,256,384]{2,1,0:T(8,128)(2,1)} fusion(bf16[256,512,1]{0,1,2:T(8,128)(2,1)S(1)} %bitcast.154, bf16[8,384,512]{2,1,0:T(8,128)(2,1)} %bitcast.153), kind=kOutput, calls=%fused_computation.16 | convolution fusion | flops 806092800 | bytes 4980736 | tf_op jit(solution)/shard_map/tk,gck->gtc/dot_general | solution.py:93
  79.7 3.8 %scatter_custom_fusion.1 = bf16[768]{0:T(1024)(128)(2,1)S(1)} fusion(s32[512]{0:T(512)S(1)} %bitcast.165, bf16[512]{0:T(512)(128)(2,1)S(1)} %reshape.350, bf16[]{:T(256)} %constant.126.clone.1), kind=kCustom, calls=%fused_computation.150 | custom fusion | bytes 1538 | tf_op jit(solution)/shard_map/scatter | solution.py:123
  86.5 27.3 %reduce-scatter.3.cloned.1.call-done = bf16[1,256,384]{2,1,0:T(8,128)(2,1)} async-done(((bf16[8,256,384]{2,1,0:T(8,128)(2,1)}), bf16[1,256,384]{2,1,0:T(8,128)(2,1)}) %reduce-scatter.3.cloned.1.call-update) | async-done | bytes 196624 | tf_op jit(solution)/shard_map/reduce_scatter | solution.py:96
  115.4 3.3 %gather_fusion = bf16[768,512]{1,0:T(8,128)(2,1)} fusion(bf16[264,512]{1,0:T(8,128)(2,1)S(1)} %concatenate.40, s32[1024]{0:T(1024)S(1)} %pad_clamp_fusion.1), kind=kCustom, calls=%fused_computation | custom fusion | bytes 1575936 | tf_op jit(solution)/shard_map/gather | solution.py:124
  122.8 11.6 %all-to-all-start = ((bf16[32,24,512]{2,1,0:T(8,128)(2,1)}), bf16[32,24,512]{2,1,0:T(8,128)(2,1)S(1)}, u32[]{:S(2)}, u32[]{:S(2)}) async-start(bf16[32,24,512]{2,1,0:T(8,128)(2,1)} %bitcast.15), calls=%async_computation.1 | async-start | bytes 1572864 | tf_op jit(solution)/shard_map/all_to_all | solution.py:126
  134.6 14.1 %all-to-all-done = bf16[32,24,512]{2,1,0:T(8,128)(2,1)S(1)} async-done(((bf16[32,24,512]{2,1,0:T(8,128)(2,1)}), bf16[32,24,512]{2,1,0:T(8,128)(2,1)S(1)}, u32[]{:S(2)}, u32[]{:S(2)}) %all-to-all-start) | async-done | bytes 786464 | tf_op jit(solution)/shard_map/all_to_all | solution.py:126
  150.0 5.0 %copy.212 = bf16[80,8,8,384]{3,2,1,0:T(8,128)(2,1)} copy(bf16[80,8,8,384]{3,1,2,0:T(8,128)(2,1)} %bitcast.151) | data formatting | bytes 7864320
  155.0 50.2 %all-gather.6.cloned.1.call-done = bf16[6208,384]{1,0:T(8,128)(2,1)} async-done(((bf16[776,384]{1,0:T(8,128)(2,1)}), bf16[6208,384]{1,0:T(8,128)(2,1)}) %all-gather.6.cloned.1.call-update) | async-done | bytes 4767760 | tf_op jit(solution)/shard_map/all_gather | solution.py:134
  206.9 7.2 %fusion.76 = f32[768,640,1]{1,0,2:T(8,128)S(1)} fusion(bf16[8,384,640]{2,1,0:T(8,128)(2,1)} %bitcast.176, bf16[8,776,384]{2,1,0:T(8,128)(2,1)} %bitcast.173, f32[8,384]{1,0:T(8,128)S(1)} %bitcast.158, f32[768]{0:T(1024)S(1)} %add_rsqrt_fusion), kind=kOutput, calls=%fused_computation.159 | convolution fusion | flops 3029336064 | bytes 10632192 | tf_op jit(solution)/shard_map/grc,gcf->rf/dot_general | solution.py:154
  214.2 4.0 %fusion.9 = bf16[768,640,1]{1,0,2:T(8,128)(2,1)S(1)} fusion(bf16[8,384,640]{2,1,0:T(8,128)(2,1)S(1)} %bitcast.177, f32[768,640,1]{1,0,2:T(8,128)S(1)} %fusion.76, bf16[8,776,384]{2,1,0:T(8,128)(2,1)S(1)} %bitcast.175, f32[8,384]{1,0:T(8,128)S(1)} %bitcast.159, f32[768]{0:T(1024)S(1)} %add_rsqrt_fusion), kind=kOutput, calls=%fused_computation.18 | convolution fusion | flops 3032285184 | bytes 11616256 | tf_op jit(solution)/shard_map/grc,gcf->rf/dot_general | solution.py:158
  218.2 5.6 %convert_bitcast_fusion = bf16[8,768,384]{2,1,0:T(8,128)(2,1)} fusion(bf16[768,640,1]{1,0,2:T(8,128)(2,1)S(1)} %fusion.9, bf16[640,8,384]{2,1,0:T(8,128)(2,1)S(1)} %bitcast.152), kind=kOutput, calls=%fused_computation.5 | convolution fusion | flops 3022258176 | bytes 9633792 | tf_op jit(solution)/shard_map/rf,fgc->grc/dot_general | solution.py:164
  224.7 4.0 %select_reduce_fusion = (f32[768]{0:T(1024)S(1)}, f32[768]{0:T(1024)S(1)}) fusion(s32[768]{0:T(1024)S(1)} %convert_reduce_fusion, pred[32]{0:T(512)(128)(4,1)S(1)} %iota_compare_fusion.4, bf16[4,8,8,384]{3,2,1,0:T(8,128)(2,1)S(1)} %bitcast.178, bf16[8,776,384]{2,1,0:T(8,128)(2,1)} %bitcast.174, f32[8,384]{1,0:T(8,128)S(1)} %bitcast.160, ...), kind=kOutput, calls=%fused_computation.97 | convolution fusion | flops 160553472 | bytes 4939808 | tf_op jit(solution)/shard_map/grc,gce->re/dot_general | solution.py:145
  229.4 53.5 %reduce-scatter.5.cloned.1.call-done = bf16[1,768,384]{2,1,0:T(8,128)(2,1)} async-done(((bf16[8,768,384]{2,1,0:T(8,128)(2,1)}), bf16[1,768,384]{2,1,0:T(8,128)(2,1)}) %reduce-scatter.5.cloned.1.call-update) | async-done | bytes 589840 | tf_op jit(solution)/shard_map/reduce_scatter | solution.py:167
  285.1 7.6 %all-to-all-start.1 = ((bf16[32,24,512]{2,1,0:T(8,128)(2,1)}), bf16[32,24,512]{2,1,0:T(8,128)(2,1)S(1)}, u32[]{:S(2)}, u32[]{:S(2)}) async-start(bf16[32,24,512]{2,1,0:T(8,128)(2,1)} %maximum_maximum_fusion), calls=%async_computation.3 | async-start | bytes 1572864 | tf_op jit(solution)/shard_map/all_to_all | solution.py:177
  292.8 14.2 %all-to-all-done.1 = bf16[32,24,512]{2,1,0:T(8,128)(2,1)S(1)} async-done(((bf16[32,24,512]{2,1,0:T(8,128)(2,1)}), bf16[32,24,512]{2,1,0:T(8,128)(2,1)S(1)}, u32[]{:S(2)}, u32[]{:S(2)}) %all-to-all-start.1) | async-done | bytes 786464 | tf_op jit(solution)/shard_map/all_to_all | solution.py:177
  (146 shorter events, 38.4 us)
Async XLA Ops:
  6.5 26.8 %copy-start = (bf16[256,512]{1,0:T(8,128)(2,1)S(1)}, bf16[256,512]{1,0:T(8,128)(2,1)}, u32[]{:S(2)}) copy-start(bf16[256,512]{1,0:T(8,128)(2,1)} %param.17) | copy-start | bytes 786436
  6.5 21.4 %copy-start.1 = (f32[4,136,128]{2,1,0:T(8,128)S(1)}, f32[4,136,128]{2,1,0:T(8,128)}, u32[]{:S(2)}) copy-start(f32[4,136,128]{2,1,0:T(8,128)} %constant.121.clone.1) | copy-start | bytes 835588
  6.5 26.8 %copy-start.5 = (bf16[256,512]{1,0:T(8,128)(2,1)S(1)}, bf16[256,512]{1,0:T(8,128)(2,1)}, u32[]{:S(2)}) copy-start(bf16[256,512]{1,0:T(8,128)(2,1)} %param.19) | copy-start | bytes 786436
  6.5 66.2 %all-gather.4.cloned.1.call-start = ((), (), s32[]{:S(2)}) async-start(), calls=%async_computation.4 | async-start | bytes 3244032 | tf_op jit(solution)/shard_map/all_gather | solution.py:90
  11.9 8.0 %collective-permute-start = (f32[4,136,128]{2,1,0:T(8,128)S(1)}, f32[4,136,128]{2,1,0:T(8,128)S(1)}, u32[]{:S(2)}, u32[]{:S(2)}) collective-permute-start(f32[4,136,128]{2,1,0:T(8,128)S(1)} %maximum_maximum_fusion.2), channel_id=1, source_target_pairs={{0,8},{8,16},{16,24},{24,32},{32,40},{40,48},{48,56},{56,64},{64,7... | collective-permute-start | bytes 835592 | tf_op jit(solution)/shard_map/ppermute | solution.py:32
  16.4 97.5 %reduce-scatter.3.cloned.1.call-start = ((), (), s32[]{:S(2)}) async-start(), calls=%async_computation.5 | async-start | bytes 1769472 | tf_op jit(solution)/shard_map/reduce_scatter | solution.py:96
  20.2 23.3 %copy-start.7 = (bf16[512]{0:T(512)(128)(2,1)S(1)}, bf16[512]{0:T(512)(128)(2,1)}, u32[]{:S(2)}) copy-start(bf16[512]{0:T(512)(128)(2,1)} %param.21) | copy-start | bytes 3076
  20.2 7.7 %collective-permute-start.1 = (f32[4,136,128]{2,1,0:T(8,128)S(1)}, f32[4,136,128]{2,1,0:T(8,128)S(1)}, u32[]{:S(2)}, u32[]{:S(2)}) collective-permute-start(f32[4,136,128]{2,1,0:T(8,128)S(1)} %maximum_maximum_fusion.3), channel_id=1, source_target_pairs={{0,16},{8,24},{16,32},{24,40},{32,48},{40,56},{48,64},{56,72},{64,... | collective-permute-start | bytes 835592 | tf_op jit(solution)/shard_map/ppermute | solution.py:32
  28.2 9.1 %collective-permute-start.2 = (f32[4,136,128]{2,1,0:T(8,128)S(1)}, f32[4,136,128]{2,1,0:T(8,128)S(1)}, u32[]{:S(2)}, u32[]{:S(2)}) collective-permute-start(f32[4,136,128]{2,1,0:T(8,128)S(1)} %maximum_maximum_fusion.4), channel_id=1, source_target_pairs={{0,32},{8,40},{16,48},{24,56},{32,64},{40,72},{48,80},{56,88},{64,... | collective-permute-start | bytes 835592 | tf_op jit(solution)/shard_map/ppermute | solution.py:32
  37.5 9.9 %collective-permute-start.3 = (f32[4,136,128]{2,1,0:T(8,128)S(1)}, f32[4,136,128]{2,1,0:T(8,128)S(1)}, u32[]{:S(2)}, u32[]{:S(2)}) collective-permute-start(f32[4,136,128]{2,1,0:T(8,128)S(1)} %maximum_maximum_fusion.5), channel_id=1, source_target_pairs={{0,64},{8,72},{16,80},{24,88},{32,96},{40,104},{48,112},{56,120},{... | collective-permute-start | bytes 835592 | tf_op jit(solution)/shard_map/ppermute | solution.py:32
  47.7 8.9 %collective-permute-start.4 = (f32[4,136,128]{2,1,0:T(8,128)S(1)}, f32[4,136,128]{2,1,0:T(8,128)S(1)}, u32[]{:S(2)}, u32[]{:S(2)}) collective-permute-start(f32[4,136,128]{2,1,0:T(8,128)S(1)} %maximum_maximum_fusion.6), channel_id=1, source_target_pairs={{0,128},{8,136},{16,144},{24,152},{32,160},{40,168},{48,176},{56,1... | collective-permute-start | bytes 835592 | tf_op jit(solution)/shard_map/ppermute | solution.py:32
  57.4 19.4 %copy-start.6 = (s32[256,2]{0,1:T(2,128)S(1)}, s32[256,2]{0,1:T(2,128)}, u32[]{:S(2)}) copy-start(s32[256,2]{0,1:T(2,128)} %param.26) | copy-start | bytes 6148
  57.6 56.3 %copy-start.3 = (bf16[256,384]{1,0:T(8,128)(2,1)S(1)}, bf16[256,384]{1,0:T(8,128)(2,1)}, u32[]{:S(2)}) copy-start(bf16[256,384]{1,0:T(8,128)(2,1)} %param.23) | copy-start | bytes 589828
  115.4 19.0 %copy-start.8 = (bf16[384]{0:T(512)(128)(2,1)S(1)}, bf16[384]{0:T(512)(128)(2,1)}, u32[]{:S(2)}) copy-start(bf16[384]{0:T(512)(128)(2,1)} %param.24) | copy-start | bytes 2308
  122.8 25.9 %all-to-all-start = ((bf16[32,24,512]{2,1,0:T(8,128)(2,1)}), bf16[32,24,512]{2,1,0:T(8,128)(2,1)S(1)}, u32[]{:S(2)}, u32[]{:S(2)}) async-start(bf16[32,24,512]{2,1,0:T(8,128)(2,1)} %bitcast.15), calls=%async_computation.1 | async-start | bytes 1572864 | tf_op jit(solution)/shard_map/all_to_all | solution.py:126
  134.4 70.8 %all-gather.6.cloned.1.call-start = ((), (), s32[]{:S(2)}) async-start(), calls=%async_computation.7 | async-start | bytes 5363712 | tf_op jit(solution)/shard_map/all_gather | solution.py:134
  150.0 133.0 %reduce-scatter.5.cloned.1.call-start = ((), (), s32[]{:S(2)}) async-start(), calls=%async_computation.6 | async-start | bytes 5308416 | tf_op jit(solution)/shard_map/reduce_scatter | solution.py:167
  206.9 7.3 %copy-start.9 = (bf16[6208,384]{1,0:T(8,128)(2,1)S(1)}, bf16[6208,384]{1,0:T(8,128)(2,1)}, u32[]{:S(2)}) copy-start(bf16[6208,384]{1,0:T(8,128)(2,1)} %all-gather.6.cloned.1.call-done) | copy-start | bytes 14303236
  206.9 7.3 %copy-start.10 = (bf16[1,3072,640]{2,1,0:T(8,128)(2,1)S(1)}, bf16[1,3072,640]{2,1,0:T(8,128)(2,1)}, u32[]{:S(2)}) copy-start(bf16[1,3072,640]{2,1,0:T(8,128)(2,1)} %param.28) | copy-start | bytes 11796484
  214.1 4.0 %copy-start.2 = (bf16[80,8,8,384]{3,2,1,0:T(8,128)(2,1)S(1)}, bf16[80,8,8,384]{3,2,1,0:T(8,128)(2,1)}, u32[]{:S(2)}) copy-start(bf16[80,8,8,384]{3,2,1,0:T(8,128)(2,1)} %copy.212) | copy-start | bytes 11796484
  223.8 0.9 copy-start.11
  285.1 21.8 %all-to-all-start.1 = ((bf16[32,24,512]{2,1,0:T(8,128)(2,1)}), bf16[32,24,512]{2,1,0:T(8,128)(2,1)S(1)}, u32[]{:S(2)}, u32[]{:S(2)}) async-start(bf16[32,24,512]{2,1,0:T(8,128)(2,1)} %maximum_maximum_fusion), calls=%async_computation.3 | async-start | bytes 1572864 | tf_op jit(solution)/shard_map/all_to_all | solution.py:177
  307.0 4.4 %copy-start.4 = (bf16[1,256,384]{2,1,0:T(8,128)(2,1)S(1)}, bf16[1,256,384]{2,1,0:T(8,128)(2,1)}, u32[]{:S(2)}) copy-start(bf16[1,256,384]{2,1,0:T(8,128)(2,1)} %reduce-scatter.3.cloned.1.call-done) | copy-start | bytes 589828
Sparse Core Ops, SparseCore 0:
  16.5 56.1 all-gather.3
  77.0 36.8 reduce-scatter.2
  150.1 55.0 all-gather.5
  224.0 58.9 reduce-scatter.4
